TPU v7x, 512 devices: a whole 4x4x16 slice. The times are simulated.
512 devices in a mesh: dp: 32 (over x, y, core), expert: 16 (over z).
Axes of the slice: x: 4, y: 4, z: 16, core: 2. Of those that a mesh axis runs over, the one named last changes fastest.
Arguments:
- out_grad: bfloat16 [65536, 2048], P(('dp', 'expert')), may hold values from -6 to 6
- expert_ids: int32 [65536, 4], P(('dp', 'expert')), may hold values from 0 to 15, all different within a row; in each aligned block of 128 rows (0 to 127, 128 to 255, ...) at most 64 rows name the same one
- route_weights: bfloat16 [65536, 4], P(('dp', 'expert')), may hold values from 0.049804688 to 1
- pre_activations: bfloat16 [65536, 4, 1536], P(('dp', 'expert')), may hold values from -6 to 6
- down_weight: bfloat16 [16, 768, 2048], P('expert', 'dp'), may hold values from -0.21875 to 0.21875
Outputs:
- pre_grad: bfloat16 [65536, 4, 1536], P(('dp', 'expert'))
- weight_grad: bfloat16 [65536, 4], P(('dp', 'expert'))
- down_grad: bfloat16 [16, 768, 2048], P('expert', 'dp')
Inputs may be any that keep to these rules, and one draw needn't show every extreme that they name: `expert_ids`: among the 128 rows of one device, each expert is named by at most 64 rows, a bound that some block reaches; the numbers in a row are distinct.
All inputs are finite; a program needn't handle non-finite values.
Results may differ from a plain program's by a relative error of at most 0.015.
Values may be sent and summed in bfloat16 or wider, within the bound.
No kernel may reach another device: no remote copies, remote signals or barrier semaphores. Data moves between devices by JAX's collectives and lax.ppermute only.
A program may use at most 64 MiB of HBM per device.

v0:
```python
import jax
import jax.numpy as jnp
from jax import lax
from jax.sharding import PartitionSpec as P

F32 = jnp.float32
BF16 = jnp.bfloat16


def body(out_grad, expert_ids, route_weights, pre_activations, down_weight):
    tok, width = out_grad.shape
    top = expert_ids.shape[1]
    units = pre_activations.shape[2] // 2
    ndp = lax.axis_size("dp")
    rows = down_weight.shape[1]
    n_all = ndp * tok
    nex = lax.axis_size("expert")
    w_all = lax.all_to_all(
        jnp.broadcast_to(down_weight, (nex,) + down_weight.shape[1:]), "expert", 0, 0, tiled=True
    )
    experts = w_all.shape[0]
    wcat = w_all.reshape(experts * rows, width)
    og_all = lax.all_gather(out_grad, "dp", axis=0, tiled=True)
    gate = pre_activations[..., :units].astype(F32)
    up = pre_activations[..., units:].astype(F32)
    sig = jax.nn.sigmoid(gate)
    hidden = (gate * sig * up).astype(BF16)
    send_h = hidden.reshape(tok, top, ndp, rows).transpose(2, 1, 3, 0)
    meta = jnp.stack([expert_ids.T.astype(BF16), route_weights.T], axis=1)
    send_h = jnp.concatenate([send_h, jnp.broadcast_to(meta[None], (ndp, top, 2, tok))], axis=2)
    got_h = lax.all_to_all(send_h, "dp", 0, 0, tiled=True)
    got_h = got_h.transpose(1, 2, 0, 3).reshape(top, rows + 2, n_all)
    hid_t = got_h[:, :rows].astype(F32)
    ids_t = got_h[:, rows].astype(F32)
    rw_t = got_h[:, rows + 1].astype(F32)
    eidx = jnp.arange(experts, dtype=F32)[:, None, None]
    hp = jnp.zeros((experts, rows, n_all), F32)
    for k in range(top):
        hp = hp + jnp.where(
            ids_t[k][None, None, :] == eidx, (rw_t[k][None, :] * hid_t[k])[None], 0.0
        )
    hp = hp.reshape(experts * rows, n_all).astype(BF16)
    part = lax.dot_general(hp, og_all, (((1,), (0,)), ((), ())), preferred_element_type=F32)
    part = (part / ndp).reshape(experts, rows, width).astype(BF16)
    down_grad = lax.psum_scatter(part, "expert", scatter_dimension=0, tiled=True)
    _, wcat = lax.optimization_barrier((part, wcat))
    r_t = lax.dot_general(wcat, og_all, (((1,), (1,)), ((), ())), preferred_element_type=F32)
    r_t = r_t.reshape(experts, rows, n_all)
    hg_t = jnp.stack(
        [jnp.sum(jnp.where(ids_t[k][None, None, :] == eidx, r_t, 0.0), axis=0) for k in range(top)]
    ).astype(BF16)
    send_g = hg_t.reshape(top, rows, ndp, tok).transpose(2, 0, 1, 3)
    got_g = lax.all_to_all(send_g, "dp", 0, 0, tiled=True)
    hidden_grad = got_g.transpose(3, 1, 0, 2).reshape(tok, top, units)
    hg32 = hidden_grad.astype(F32)
    weight_grad = jnp.sum(hg32 * hidden.astype(F32), axis=-1).astype(BF16)
    cot = route_weights.astype(F32)[..., None] * hg32
    gate_grad = cot * up * sig * (1.0 + gate * (1.0 - sig))
    up_grad = cot * gate * sig
    pre_grad = jnp.concatenate([gate_grad, up_grad], axis=-1).astype(BF16)
    return (pre_grad, weight_grad, down_grad)


def solution(mesh):
    return jax.shard_map(
        body,
        mesh=mesh,
        in_specs=(
            P(("dp", "expert"), None),
            P(("dp", "expert"), None),
            P(("dp", "expert"), None),
            P(("dp", "expert"), None, None),
            P("expert", "dp", None),
        ),
        out_specs=(
            P(("dp", "expert"), None, None),
            P(("dp", "expert"), None),
            P("expert", "dp", None),
        ),
        check_vma=False,
    )
```

profile of v0, /device:TPU:2, one launch (start us, length us, event | category | flops | bytes accessed | tf_op | source)
XLA Modules:
  0.0 194.8 jit_solution(4540025526134113326)
XLA Ops:
  7.2 0.0 all-gather.2.cloned.1.call-start
  7.2 0.7 all-gather.2.cloned.1.call-update
  7.9 1.9 fusion.11
  9.8 0.0 copy-start.2
  9.8 0.0 copy-start.1
  9.8 0.7 copy.28
  10.5 0.7 copy.29
  11.2 0.0 copy-done.2
  11.2 0.0 copy-done.1
  11.2 0.5 fusion
  11.8 0.1 pad_maximum_fusion.1
  11.9 0.0 copy-start
  11.9 0.7 copy.19
  12.6 21.3 %all_to_all.15 = bf16[32,4,26,128]{3,1,2,0:T(4,128)(2,1)S(1)} all-to-all(bf16[32,4,26,128]{3,1,2,0:T(4,128)(2,1)S(1)} %copy.19), channel_id=1, replica_groups=mesh['dp'=32,'expert'=16] {'dp'}, dimensions={0} | all-to-all | bytes 1703936 | tf_op jit(solution)/shard_map/all_to_all | solution.py:31
  33.9 0.0 copy-done
  33.9 1.3 broadcast_in_dim.115
  35.3 14.0 %all-to-all-start.1 = ((bf16[16,24,2048]{2,1,0:T(8,128)(2,1)}), bf16[16,24,2048]{2,1,0:T(8,128)(2,1)}, u32[]{:S(2)}, u32[]{:S(2)}) async-start(bf16[16,24,2048]{2,1,0:T(8,128)(2,1)} %broadcast_in_dim.115), calls=%async_computation.1 | async-start | bytes 3145728 | tf_op jit(solution)/shard_map/all_to_all | solution.py:18
  49.3 0.0 reduce-scatter.2.cloned.1.call-start
  49.3 0.4 copy_bitcast_fusion
  49.8 0.1 fusion.12
  49.9 0.2 slice_convert_fusion
  50.1 1.8 slice_multiply_fusion.3
  51.9 0.2 copy.43
  52.2 0.2 copy.44
  52.4 0.2 copy.45
  52.6 0.2 copy.46
  53.0 4.3 %add_convert_fusion = bf16[16,24,4096]{2,1,0:T(8,128)(2,1)} fusion(f32[24,4096]{1,0:T(8,128)S(1)} %bitcast.82, f32[24,4096]{1,0:T(8,128)S(1)} %bitcast.83, f32[24,4096]{1,0:T(8,128)S(1)} %bitcast.84, f32[24,4096]{1,0:T(8,128)S(1)} %bitcast.85, pred[16,4096]{1,0:T(8,128)(4,1)S(1)} %iota_compare_fusion, pred[16,4096]{1,0:T(8,128)(4,1)S(1)} %iota_compare_fusion.1, ...), kind=kLoop, calls=%fused_computation.4 | loop fusion | flops 12582912 | bytes 4980736 | tf_op jit(solution)/shard_map/convert.12
  57.3 46.1 %all-gather.2.cloned.1.call-done = bf16[4096,2048]{1,0:T(8,128)(2,1)} async-done(((bf16[128,2048]{1,0:T(8,128)(2,1)}), bf16[4096,2048]{1,0:T(8,128)(2,1)}) %all-gather.2.cloned.1.call-update) | async-done | bytes 16777232 | tf_op jit(solution)/shard_map/all_gather | solution.py:23
  103.4 12.0 %multiply_convert_fusion = bf16[384,2048]{1,0:T(8,128)(2,1)} fusion(bf16[384,4096]{1,0:T(8,128)(2,1)} %bitcast.80, bf16[4096,2048]{1,0:T(8,128)(2,1)} %all-gather.2.cloned.1.call-done), kind=kOutput, calls=%fused_computation.5 | convolution fusion | flops 6444023808 | bytes 21495808 | tf_op jit(solution)/shard_map/dot_general | solution.py:43
  115.5 0.0 reduce-scatter.2.cloned.1.call-update
  115.5 5.9 %all-to-all-done.1 = bf16[16,24,2048]{2,1,0:T(8,128)(2,1)} async-done(((bf16[16,24,2048]{2,1,0:T(8,128)(2,1)}), bf16[16,24,2048]{2,1,0:T(8,128)(2,1)}, u32[]{:S(2)}, u32[]{:S(2)}) %all-to-all-start.1) | async-done | bytes 1572896 | tf_op jit(solution)/shard_map/all_to_all | solution.py:18
  121.4 10.7 %fusion.14 = f32[384,4096]{1,0:T(8,128)S(1)} fusion(bf16[384,2048]{1,0:T(8,128)(2,1)} %bitcast.18, bf16[4096,2048]{1,0:T(8,128)(2,1)} %all-gather.2.cloned.1.call-done), kind=kOutput, calls=%fused_computation.53 | convolution fusion | flops 6442450944 | bytes 24641536 | tf_op jit(solution)/shard_map/dot_general | solution.py:47
  132.1 3.4 %select_reduce_fusion.3 = (bf16[24,4096]{1,0:T(8,128)(2,1)S(1)}, bf16[24,4096]{1,0:T(8,128)(2,1)S(1)}, bf16[24,4096]{1,0:T(8,128)(2,1)S(1)}, bf16[24,4096]{1,0:T(8,128)(2,1)S(1)}) fusion(f32[16,24,4096]{2,1,0:T(8,128)S(1)} %bitcast.79, pred[16,4096]{1,0:T(8,128)(4,1)S(1)} %iota_compare_fusion.3, pred[16,4096]{1,0:T(8,128)(4,1)S(1)} %iota_compare_fusion, ...), kind=kLoop, calls=%fused_computation.3 | loop fusion | flops 12189696 | bytes 7340032 | tf_op jit(solution)/shard_map/reduce_sum | solution.py:50
  135.6 0.1 maximum_bitcast_fusion
  135.8 1.2 copy.21
  136.9 8.1 %all-to-all-start.2 = ((bf16[32,4,24,128]{3,2,1,0:T(8,128)(2,1)}), bf16[32,4,24,128]{3,2,1,0:T(8,128)(2,1)S(1)}, u32[]{:S(2)}, u32[]{:S(2)}) async-start(bf16[32,4,24,128]{3,2,1,0:T(8,128)(2,1)} %copy.21), calls=%async_computation.2 | async-start | bytes 1572864 | tf_op jit(solution)/shard_map/all_to_all | solution.py:53
  145.0 12.0 %all-to-all-done.2 = bf16[32,4,24,128]{3,2,1,0:T(8,128)(2,1)S(1)} async-done(((bf16[32,4,24,128]{3,2,1,0:T(8,128)(2,1)}), bf16[32,4,24,128]{3,2,1,0:T(8,128)(2,1)S(1)}, u32[]{:S(2)}, u32[]{:S(2)}) %all-to-all-start.2) | async-done | bytes 786464 | tf_op jit(solution)/shard_map/all_to_all | solution.py:53
  157.1 1.6 fusion.3
  158.7 0.1 pad_maximum_fusion
  158.8 2.5 %copy.23 = bf16[128,4,1536]{2,1,0:T(4,128)(2,1)} copy(bf16[128,4,1536]{0,2,1:T(8,128)(2,1)S(1)} %pad_maximum_fusion) | data formatting | bytes 3145728
  161.3 26.6 %reduce-scatter.2.cloned.1.call-done = bf16[1,24,2048]{2,1,0:T(8,128)(2,1)} async-done(((bf16[16,24,2048]{2,1,0:T(8,128)(2,1)}), bf16[1,24,2048]{2,1,0:T(8,128)(2,1)}) %reduce-scatter.2.cloned.1.call-update) | async-done | bytes 98320 | tf_op jit(solution)/shard_map/reduce_scatter | solution.py:45
  (14 shorter events, 0.4 us)
Async XLA Ops:
  7.2 96.3 %all-gather.2.cloned.1.call-start = ((), (), s32[]{:S(2)}) async-start(), calls=%async_computation.4 | async-start | bytes 17301504 | tf_op jit(solution)/shard_map/all_gather | solution.py:23
  9.8 1.4 copy-start.2
  9.8 1.4 copy-start.1
  11.9 22.0 %copy-start = (bf16[1,24,2048]{2,1,0:T(8,128)(2,1)S(1)}, bf16[1,24,2048]{2,1,0:T(8,128)(2,1)}, u32[]{:S(2)}) copy-start(bf16[1,24,2048]{2,1,0:T(8,128)(2,1)} %param.9) | copy-start | bytes 294916
  35.3 86.2 %all-to-all-start.1 = ((bf16[16,24,2048]{2,1,0:T(8,128)(2,1)}), bf16[16,24,2048]{2,1,0:T(8,128)(2,1)}, u32[]{:S(2)}, u32[]{:S(2)}) async-start(bf16[16,24,2048]{2,1,0:T(8,128)(2,1)} %broadcast_in_dim.115), calls=%async_computation.1 | async-start | bytes 3145728 | tf_op jit(solution)/shard_map/all_to_all | solution.py:18
  49.3 138.6 %reduce-scatter.2.cloned.1.call-start = ((), (), s32[]{:S(2)}) async-start(), calls=%async_computation.5 | async-start | bytes 1671168 | tf_op jit(solution)/shard_map/reduce_scatter | solution.py:45
  136.9 20.1 %all-to-all-start.2 = ((bf16[32,4,24,128]{3,2,1,0:T(8,128)(2,1)}), bf16[32,4,24,128]{3,2,1,0:T(8,128)(2,1)S(1)}, u32[]{:S(2)}, u32[]{:S(2)}) async-start(bf16[32,4,24,128]{3,2,1,0:T(8,128)(2,1)} %copy.21), calls=%async_computation.2 | async-start | bytes 1572864 | tf_op jit(solution)/shard_map/all_to_all | solution.py:53
Sparse Core Ops, SparseCore 0:
  11.1 92.2 all-gather.1
  115.6 72.2 reduce-scatter.1
where the time goes:
time: 195 us
  waiting for transfers between devices  91.4 us (47%)
  matrix products  22.7 us (12%)
  starting transfers between devices  22.2 us (11%)
  blocking collectives  21.3 us (11%)
  between operations  14.3 us (7%)
  other arithmetic  12.3 us (6%)
  local copies, waits for them, and re-layouts  10.5 us (5%)
    all_gather x1, waiting for transfers between devices, body(): og_all = lax.all_gather(out_grad, 'dp', axis=0, tiled=True)  46.1 us
    reduce_scatter x1, waiting for transfers between devices, body(): lax.psum_scatter(part, 'expert', scatter_dimension=0, tiled=True)  26.6 us
    all_to_all x1, blocking collectives, body(): got_h = lax.all_to_all(send_h, 'dp', 0, 0, tiled=True)  21.3 us
    all_to_all x1, starting transfers between devices, body(): lax.all_to_all(jnp.broadcast_to(down_weight, (nex,) + down_weight.shape[1...  14 us
    all_to_all x1, waiting for transfers between devices, body(): got_g = lax.all_to_all(send_g, 'dp', 0, 0, tiled=True)  12 us
    dot_general x1, matrix products, body(): lax.dot_general(hp, og_all, (((1,), (0,)), ((), ())), preferred_element_t...  12 us
    dot_general x1, matrix products, body(): lax.dot_general(wcat, og_all, (((1,), (1,)), ((), ())), preferred_element...  10.7 us
    all_to_all x1, starting transfers between devices, body(): got_g = lax.all_to_all(send_g, 'dp', 0, 0, tiled=True)  8.07 us
  transfers between devices with their start and end apart: 4, of which 4 were waited for; matrix products, arithmetic and copies ran while one was open for 23% of the time, Pallas kernels for 0%

commit v1 on v0

--- a/solution.py
+++ b/solution.py
@@ -20,7 +20,10 @@
     )
     experts = w_all.shape[0]
     wcat = w_all.reshape(experts * rows, width)
-    og_all = lax.all_gather(out_grad, "dp", axis=0, tiled=True)
+    refer_inputs = lambda v0: jnp.concatenate(
+        lax.all_to_all(jnp.stack([v0 for _ in range(lax.axis_size("dp"))], 0), "dp", 0, 0), 0
+    )
+    og_all = refer_inputs(out_grad)
     gate = pre_activations[..., :units].astype(F32)
     up = pre_activations[..., units:].astype(F32)
     sig = jax.nn.sigmoid(gate)

time: 195 us -> 456 us (2.34)
  the two profiles are of different devices: /device:TPU:2 before, /device:TPU:1 now
where the time goes in v1:
time: 456 us; the launch traced here: 455 us
  waiting for transfers between devices  289 us (63%)
  starting transfers between devices  74.5 us (16%)
  blocking collectives  24.5 us (5%)
  matrix products  24.4 us (5%)
  local copies, waits for them, and re-layouts  19 us (4%)
  between operations  14.4 us (3%)
  other arithmetic  9.08 us (2%)
    all_to_all x1, waiting for transfers between devices, body(): lax.all_to_all(jnp.stack([v0 for _ in range(lax.axis_size('dp'))], 0), 'd...  227 us
    all_to_all x1, starting transfers between devices, body(): got_g = lax.all_to_all(send_g, 'dp', 0, 0, tiled=True)  56 us
    all_to_all x1, waiting for transfers between devices, body(): lax.all_to_all(jnp.broadcast_to(down_weight, (nex,) + down_weight.shape[1...  47.8 us
    all_to_all x1, blocking collectives, body(): got_h = lax.all_to_all(send_h, 'dp', 0, 0, tiled=True)  24.5 us
    all_to_all x1, waiting for transfers between devices, body(): got_g = lax.all_to_all(send_g, 'dp', 0, 0, tiled=True)  14.2 us
    all_to_all x1, starting transfers between devices, body(): lax.all_to_all(jnp.broadcast_to(down_weight, (nex,) + down_weight.shape[1...  13.4 us
    dot_general x1, matrix products, body(): lax.dot_general(wcat, og_all, (((1,), (1,)), ((), ())), preferred_element...  12.7 us
    dot_general x1, matrix products, body(): lax.dot_general(hp, og_all, (((1,), (0,)), ((), ())), preferred_element_t...  11.6 us
  transfers between devices with their start and end apart: 4, of which 3 were waited for; matrix products, arithmetic and copies ran while one was open for 9% of the time, Pallas kernels for 0%

profile of v1, /device:TPU:1, one launch (start us, length us, event | category | flops | bytes accessed | tf_op | source)
XLA Modules:
  0.0 455.1 jit_solution(16671607058256804401)
XLA Ops:
  7.2 1.9 fusion.11
  9.1 0.0 copy-start.7
  9.1 0.0 copy-start.5
  9.1 0.7 copy.29
  9.8 0.7 copy.30
  10.5 0.0 copy-done.7
  10.5 0.0 copy-done.5
  10.5 0.5 fusion
  11.0 0.1 pad_maximum_fusion.1
  11.2 0.0 copy-start
  11.2 0.7 copy.20
  11.9 24.5 %all_to_all.20 = bf16[32,4,26,128]{3,1,2,0:T(4,128)(2,1)S(1)} all-to-all(bf16[32,4,26,128]{3,1,2,0:T(4,128)(2,1)S(1)} %copy.20), channel_id=1, replica_groups=mesh['dp'=32,'expert'=16] {'dp'}, dimensions={0} | all-to-all | bytes 1703936 | tf_op jit(solution)/shard_map/all_to_all | solution.py:34
  36.4 0.0 copy-done
  36.4 5.9 %stack.21 = bf16[32,128,2048]{2,1,0:T(8,128)(2,1)} broadcast(bf16[128,2048]{1,0:T(8,128)(2,1)S(1)} %copy-done), dimensions={1,2} | broadcast | bytes 17301504 | tf_op jit(solution)/shard_map/stack | solution.py:24
  42.3 5.0 %all-to-all-start.1 = ((bf16[32,128,2048]{2,1,0:T(8,128)(2,1)}), bf16[32,128,2048]{2,1,0:T(8,128)(2,1)}, u32[]{:S(2)}, u32[]{:S(2)}) async-start(bf16[32,128,2048]{2,1,0:T(8,128)(2,1)} %stack.21), calls=%async_computation.1 | async-start | bytes 33554432 | tf_op jit(solution)/shard_map/all_to_all | solution.py:24
  47.2 0.4 copy_bitcast_fusion
  47.7 0.7 fusion.12
  48.4 0.2 slice_convert_fusion
  48.6 2.6 slice_multiply_fusion.3
  51.1 227.3 %all-to-all-done.1 = bf16[32,128,2048]{2,1,0:T(8,128)(2,1)} async-done(((bf16[32,128,2048]{2,1,0:T(8,128)(2,1)}), bf16[32,128,2048]{2,1,0:T(8,128)(2,1)}, u32[]{:S(2)}, u32[]{:S(2)}) %all-to-all-start.1) | async-done | bytes 16777248 | tf_op jit(solution)/shard_map/all_to_all | solution.py:24
  278.4 2.2 broadcast_in_dim.115
  280.7 13.4 %all-to-all-start.2 = ((bf16[16,24,2048]{2,1,0:T(8,128)(2,1)}), bf16[16,24,2048]{2,1,0:T(8,128)(2,1)}, u32[]{:S(2)}, u32[]{:S(2)}) async-start(bf16[16,24,2048]{2,1,0:T(8,128)(2,1)} %broadcast_in_dim.115), calls=%async_computation.2 | async-start | bytes 3145728 | tf_op jit(solution)/shard_map/all_to_all | solution.py:18
  294.0 0.2 reduce-scatter.2.cloned.1.call-start
  294.3 0.8 iota_compare_fusion
  295.0 0.0 copy-start.1
  295.0 0.0 copy-start.4
  295.0 0.0 copy-start.3
  295.1 1.3 copy.44
  296.3 0.2 copy.45
  296.6 0.2 copy.46
  296.8 0.2 copy.47
  297.0 0.0 copy-done.4
  297.1 0.0 copy-done.3
  297.2 0.0 copy-done.1
  297.2 3.0 add_convert_fusion
  300.2 11.6 %multiply_convert_fusion = bf16[384,2048]{1,0:T(8,128)(2,1)} fusion(bf16[384,4096]{1,0:T(8,128)(2,1)S(1)} %bitcast.82, bf16[4096,2048]{1,0:T(8,128)(2,1)} %bitcast.16), kind=kOutput, calls=%fused_computation.5 | convolution fusion | flops 6444023808 | bytes 21495808 | tf_op jit(solution)/shard_map/dot_general | solution.py:46
  311.8 0.0 reduce-scatter.2.cloned.1.call-update
  311.9 47.8 %all-to-all-done.2 = bf16[16,24,2048]{2,1,0:T(8,128)(2,1)} async-done(((bf16[16,24,2048]{2,1,0:T(8,128)(2,1)}), bf16[16,24,2048]{2,1,0:T(8,128)(2,1)}, u32[]{:S(2)}, u32[]{:S(2)}) %all-to-all-start.2) | async-done | bytes 1572896 | tf_op jit(solution)/shard_map/all_to_all | solution.py:18
  359.6 12.7 %select_reduce_fusion.3 = (bf16[24,4096]{1,0:T(8,128)(2,1)S(1)}, bf16[24,4096]{1,0:T(8,128)(2,1)S(1)}, bf16[24,4096]{1,0:T(8,128)(2,1)S(1)}, bf16[24,4096]{1,0:T(8,128)(2,1)S(1)}) fusion(pred[16,4096]{1,0:T(8,128)(4,1)S(1)} %iota_compare_fusion.3, pred[16,4096]{1,0:T(8,128)(4,1)S(1)} %copy-done.2, pred[16,4096]{1,0:T(8,128)(4,1)S(1)} %iota_compare_fusion.1, ...), kind=kOutput, calls=%fused_computation.3 | convolution fusion | flops 6454640640 | bytes 19398656 | tf_op jit(solution)/shard_map/dot_general | solution.py:50
  372.5 0.1 maximum_bitcast_fusion
  372.6 0.0 copy-start.6
  372.6 1.2 copy.22
  373.8 56.0 %all-to-all-start.3 = ((bf16[32,4,24,128]{3,2,1,0:T(8,128)(2,1)}), bf16[32,4,24,128]{3,2,1,0:T(8,128)(2,1)S(1)}, u32[]{:S(2)}, u32[]{:S(2)}) async-start(bf16[32,4,24,128]{3,2,1,0:T(8,128)(2,1)} %copy.22), calls=%async_computation.3 | async-start | bytes 1572864 | tf_op jit(solution)/shard_map/all_to_all | solution.py:56
  429.8 0.0 copy-done.6
  429.8 14.2 %all-to-all-done.3 = bf16[32,4,24,128]{3,2,1,0:T(8,128)(2,1)S(1)} async-done(((bf16[32,4,24,128]{3,2,1,0:T(8,128)(2,1)}), bf16[32,4,24,128]{3,2,1,0:T(8,128)(2,1)S(1)}, u32[]{:S(2)}, u32[]{:S(2)}) %all-to-all-start.3) | async-done | bytes 786464 | tf_op jit(solution)/shard_map/all_to_all | solution.py:56
  444.0 1.6 fusion.3
  445.7 0.1 pad_maximum_fusion
  445.8 2.5 copy.24
  (16 shorter events, 0.3 us)
Async XLA Ops:
  9.1 1.4 copy-start.7
  9.1 1.4 copy-start.5
  11.2 25.2 %copy-start = (bf16[128,2048]{1,0:T(8,128)(2,1)S(1)}, bf16[128,2048]{1,0:T(8,128)(2,1)}, u32[]{:S(2)}) copy-start(bf16[128,2048]{1,0:T(8,128)(2,1)} %param.5) | copy-start | bytes 1572868
  42.3 236.2 %all-to-all-start.1 = ((bf16[32,128,2048]{2,1,0:T(8,128)(2,1)}), bf16[32,128,2048]{2,1,0:T(8,128)(2,1)}, u32[]{:S(2)}, u32[]{:S(2)}) async-start(bf16[32,128,2048]{2,1,0:T(8,128)(2,1)} %stack.21), calls=%async_computation.1 | async-start | bytes 33554432 | tf_op jit(solution)/shard_map/all_to_all | solution.py:24
  280.7 79.0 %all-to-all-start.2 = ((bf16[16,24,2048]{2,1,0:T(8,128)(2,1)}), bf16[16,24,2048]{2,1,0:T(8,128)(2,1)}, u32[]{:S(2)}, u32[]{:S(2)}) async-start(bf16[16,24,2048]{2,1,0:T(8,128)(2,1)} %broadcast_in_dim.115), calls=%async_computation.2 | async-start | bytes 3145728 | tf_op jit(solution)/shard_map/all_to_all | solution.py:18
  294.0 154.2 %reduce-scatter.2.cloned.1.call-start = ((), (), s32[]{:S(2)}) async-start(), calls=%async_computation.5 | async-start | bytes 1671168 | tf_op jit(solution)/shard_map/reduce_scatter | solution.py:48
  295.0 2.2 copy-start.1
  295.0 2.0 copy-start.4
  295.0 2.1 copy-start.3
  311.8 47.8 %copy-start.2 = (pred[16,4096]{1,0:T(8,128)(4,1)S(1)}, pred[16,4096]{1,0:T(8,128)(4,1)}, u32[]{:S(2)}) copy-start(pred[16,4096]{1,0:T(8,128)(4,1)} %copy-done.1) | copy-start | bytes 196612
  372.6 57.2 %copy-start.6 = (bf16[128,4]{0,1:T(4,128)(2,1)S(1)}, bf16[128,4]{0,1:T(4,128)(2,1)}, u32[]{:S(2)}) copy-start(bf16[128,4]{0,1:T(4,128)(2,1)} %param.7) | copy-start | bytes 3076
  373.8 70.2 %all-to-all-start.3 = ((bf16[32,4,24,128]{3,2,1,0:T(8,128)(2,1)}), bf16[32,4,24,128]{3,2,1,0:T(8,128)(2,1)S(1)}, u32[]{:S(2)}, u32[]{:S(2)}) async-start(bf16[32,4,24,128]{3,2,1,0:T(8,128)(2,1)} %copy.22), calls=%async_computation.3 | async-start | bytes 1572864 | tf_op jit(solution)/shard_map/all_to_all | solution.py:56
Sparse Core Ops, SparseCore 0:
  312.0 99.7 reduce-scatter.1
